TPU v7x, 256 devices: a whole 4x4x8 slice. The times are simulated.
256 devices in a mesh: tok: 32 (over z, x), head: 8 (over y, core).
Axes of the slice: x: 4, y: 4, z: 8, core: 2. Of those that a mesh axis runs over, the one named last changes fastest.
Arguments:
- embeddings: bfloat16 [4096, 4096], P('tok'), may hold values from -6 to 6
- norm_gain: bfloat16 [4096], replicated, may hold values from 0.099609375 to 1.8984375
- query_key_value_weight: bfloat16 [4096, 6144], P(None, 'head'), may hold values from -0.09375 to 0.09375
- embed_table: bfloat16 [65536, 4096], P('tok', 'head'), may hold values from -6 to 6
- rotated_cache_pages: bfloat16 [32, 32, 256, 2048], P('tok', None, None, 'head'), may hold values from -300 to 300
- page_owner_device: int32 [32, 32], P('tok'), may hold values from 0 to 31, each once within a row
- cached_length: int32 [32], P('tok'), may hold values from 2 to 8192, as said below
- vocab_shard: int32 [4096, 1], P('tok'), may hold values from 0 to 31; in each aligned block of 128 rows (0 to 127, 128 to 255, ...) at most 8 rows name the same one
- shard_row: int32 [4096], P('tok'), may hold values from 0 to 2047
- accept: int32 [4096], P('tok'), may hold values from 0 to 1, as said below
Outputs:
- out_first: bfloat16 [4096, 4096], P('tok', 'head')
- out_second: bfloat16 [4096, 4096], P('tok', 'head')
Inputs may be any that keep to these rules, and one draw needn't show every extreme that they name: `page_owner_device`: each row names every device of the tok axis once. `cached_length`: some request has exactly 8192 cached positions. `vocab_shard`: at most 8 of the 128 tokens of one request name the same shard, and some shard is named that often. `accept`: at most 32 accepted tokens in one request's block; some block has exactly 32.
All inputs are finite; a program needn't handle non-finite values.
Results may differ from a plain program's by a relative error of at most 0.017.
The roundings to bfloat16 on the way count: a program that leaves them out, or rounds other values in their place, can miss the bound.
Values may be sent and summed in bfloat16 or wider, within the bound.
No kernel may reach another device: no remote copies, remote signals or barrier semaphores. Data moves between devices by JAX's collectives and lax.ppermute only.
A program may use at most 128 MiB of HBM per device.

v0:
```python
import math
import jax
import jax.numpy as jnp
from jax import lax
from jax.sharding import PartitionSpec as P

QUERY_HEADS = 32
KEY_VALUE_HEADS = 8
HEAD_SIZE = 128
THETA = 500000.0


def angles(positions):
    steps_half = jnp.arange(HEAD_SIZE // 2, dtype=jnp.float32)
    frequency = THETA ** (-(steps_half * 2.0) / HEAD_SIZE)
    return positions.astype(jnp.float32)[:, None] * frequency[None, :]


def rotate(vectors, turning):
    half_width = vectors.shape[-1] // 2
    former = vectors[..., :half_width]
    latter = vectors[..., half_width:]
    cosine = jnp.cos(turning)
    sine_of = jnp.sin(turning)
    return jnp.concatenate(
        [former * cosine - latter * sine_of, latter * cosine + former * sine_of], axis=-1
    )


def project(inputs, norm_gain, query_key_value_weight, positions):
    widened = inputs.astype(jnp.float32)
    inverse = lax.rsqrt(jnp.mean(widened * widened, axis=-1, keepdims=True) + 1e-05)
    normed = (widened * inverse * norm_gain.astype(jnp.float32)).astype(jnp.bfloat16)
    combined = jnp.dot(normed, query_key_value_weight, preferred_element_type=jnp.float32)
    heads_per_group = QUERY_HEADS // KEY_VALUE_HEADS
    combined = combined.reshape(inputs.shape[0], -1, heads_per_group + 2, HEAD_SIZE)
    turning = angles(positions)[:, None, None, :]
    query_vectors = rotate(combined[:, :, :heads_per_group], turning).astype(jnp.bfloat16)
    block_keys = rotate(combined[:, :, heads_per_group : heads_per_group + 1], turning)[
        :, :, 0
    ].astype(jnp.bfloat16)
    block_values = combined[:, :, heads_per_group + 1].astype(jnp.bfloat16)
    return (query_vectors, block_keys, block_values)


def attend(query_vectors, block_keys, block_values, page_keys, page_values, usable):
    factor = 1.0 / math.sqrt(HEAD_SIZE)
    scores_cache = (
        jnp.einsum("bgqd,kgd->gqbk", query_vectors, page_keys, preferred_element_type=jnp.float32)
        * factor
    )
    scores_cache = jnp.where(usable[None, None, None, :], scores_cache, -1e30)
    scores_block = (
        jnp.einsum("bgqd,cgd->gqbc", query_vectors, block_keys, preferred_element_type=jnp.float32)
        * factor
    )
    highest = jnp.maximum(jnp.max(scores_cache, axis=-1), jnp.max(scores_block, axis=-1))[..., None]
    exp_cache = jnp.exp(scores_cache - highest)
    exp_block = jnp.exp(scores_block - highest)
    totals = jnp.sum(exp_cache, axis=-1) + jnp.sum(exp_block, axis=-1)
    weights_cache = exp_cache.astype(jnp.bfloat16)
    weights_block = exp_block.astype(jnp.bfloat16)
    combined = jnp.einsum(
        "gqbk,kgd->bgqd", weights_cache, page_values, preferred_element_type=jnp.float32
    )
    combined = combined + jnp.einsum(
        "gqbc,cgd->bgqd", weights_block, block_values, preferred_element_type=jnp.float32
    )
    result = combined / jnp.transpose(totals, (2, 0, 1))[..., None]
    return result.astype(jnp.bfloat16).reshape(query_vectors.shape[0], -1)


def body(
    embeddings,
    norm_gain,
    query_key_value_weight,
    embed_table,
    rotated_cache_pages,
    page_owner_device,
    cached_length,
    vocab_shard,
    shard_row,
    accept,
):
    members = lax.axis_size("tok")
    length = embeddings.shape[0]
    sources = jnp.arange(members, dtype=jnp.int32)
    positions = cached_length[0] + jnp.arange(length, dtype=jnp.int32)
    query_vectors, block_keys, block_values = project(
        embeddings, norm_gain, query_key_value_weight, positions
    )
    arrived = lax.all_to_all(rotated_cache_pages, "tok", split_axis=1, concat_axis=0, tiled=True)
    page_size = arrived.shape[2]
    arrived = arrived.reshape(members * page_size, -1, 2, HEAD_SIZE)
    page_index = jnp.sum(
        jnp.where(page_owner_device[0][:, None] == sources[None, :], sources[:, None], 0), axis=0
    )
    page_spots = page_index[:, None] * page_size + jnp.arange(page_size, dtype=jnp.int32)[None, :]
    usable = page_spots.reshape(-1) < cached_length[0]
    page_keys = arrived[:, :, 0]
    page_values = arrived[:, :, 1]

    def run_attention(query_rows, key_rows, value_rows):
        return attend(query_rows, key_rows, value_rows, page_keys, page_values, usable)

    output_one = run_attention(query_vectors, block_keys, block_values)
    target_shard = vocab_shard[:, 0]
    capacity = max(2, 2 * length // members)
    chosen = (target_shard[:, None] == sources[None, :]).astype(jnp.int32)
    earlier = (jnp.arange(length)[:, None] > jnp.arange(length)[None, :]).astype(jnp.int32)
    slot_rank = jnp.sum(jnp.dot(earlier, chosen) * chosen, axis=1)
    wanted = jnp.zeros((members, capacity), jnp.int32).at[target_shard, slot_rank].set(shard_row)
    found_rows = jnp.take(
        embed_table, lax.all_to_all(wanted, "tok", split_axis=0, concat_axis=0, tiled=True), axis=0
    )
    returned = lax.all_to_all(found_rows, "tok", split_axis=0, concat_axis=0, tiled=True)
    replacement = returned[target_shard, slot_rank]
    full_rows = lax.all_gather(replacement, "head", axis=1, tiled=True)
    replaced = jnp.where(accept[:, None] == 1, full_rows, embeddings)
    queries_two, keys_two, values_two = project(
        replaced, norm_gain, query_key_value_weight, positions
    )
    output_two = run_attention(queries_two, keys_two, values_two)
    return (output_one, output_two)


def solution(mesh):
    return jax.shard_map(
        body,
        mesh=mesh,
        in_specs=(
            P("tok", None),
            P(),
            P(None, "head"),
            P("tok", "head"),
            P("tok", None, None, "head"),
            P("tok", None),
            P("tok"),
            P("tok", None),
            P("tok"),
            P("tok"),
        ),
        out_specs=(P("tok", "head"), P("tok", "head")),
        check_vma=False,
    )
```

profile of v0, /device:TPU:12, one launch (start us, length us, event | category | flops | bytes accessed | tf_op | source)
XLA Modules:
  0.0 241.9 jit_solution(14365437352633551345)
XLA Ops:
  7.2 1.0 fusion.36
  8.8 10.9 %scatter_fusion = s32[32,8]{0,1:T(8,128)S(1)} fusion(s32[32,8]{0,1:T(8,128)S(1)} %broadcast_in_dim.55, s32[128]{0:T(128)S(1)} %get-tuple-element.14, s32[128]{0:T(128)} %param.18), kind=kCustom, calls=%fused_computation.2 | custom fusion | bytes 2560 | tf_op jit(solution)/shard_map/scatter | solution.py:112
  19.9 19.1 %all_to_all.29 = s32[32,1,8]{2,1,0:T(1,128)S(1)} all-to-all(s32[32,1,8]{2,1,0:T(1,128)S(1)} %copy.91), channel_id=1, replica_groups=mesh['tok'=32,'head'=8] {'tok'}, dimensions={0} | all-to-all | bytes 2048 | tf_op jit(solution)/shard_map/all_to_all | solution.py:114
  39.3 1.2 gather_fusion
  40.5 15.1 %all_to_all.30 = bf16[32,8,512]{2,1,0:T(8,128)(2,1)S(1)} all-to-all(bf16[32,8,512]{2,1,0:T(8,128)(2,1)S(1)} %bitcast_select_fusion.2), channel_id=1, replica_groups=mesh['tok'=32,'head'=8] {'tok'}, dimensions={0} | all-to-all | bytes 524288 | tf_op jit(solution)/shard_map/all_to_all | solution.py:116
  55.6 6.6 %all-to-all-start = ((bf16[1,32,256,256]{3,2,0,1:T(8,128)(2,1)}), bf16[1,32,256,256]{3,2,0,1:T(8,128)(2,1)}, u32[]{:S(2)}, u32[]{:S(2)}) async-start(bf16[1,32,256,256]{3,2,0,1:T(8,128)(2,1)} %bitcast.163), calls=%async_computation | async-start | bytes 8388608 | tf_op jit(solution)/shard_map/all_to_all | solution.py:92
  62.3 1.9 gather_fusion.1
  65.5 25.3 %all-gather.2.cloned.1.call-done = bf16[128,4096]{1,0:T(8,128)(2,1)} async-done(((bf16[128,512]{1,0:T(8,128)(2,1)}), bf16[128,4096]{1,0:T(8,128)(2,1)}) %all-gather.2.cloned.1.call-update) | async-done | bytes 1048592 | tf_op jit(solution)/shard_map/all_gather | solution.py:118
  90.8 1.9 fusion.17
  92.7 5.8 %fusion.41 = f32[128,768]{0,1:T(8,128)S(1)} fusion(bf16[4096,768]{1,0:T(8,128)(2,1)} %param.12, f32[128]{0:T(128)S(1)} %get-tuple-element.44, f32[4096]{0:T(1024)S(1)} %convert_element_type.83, bf16[128,4096]{1,0:T(8,128)(2,1)} %all-gather.2.cloned.1.call-done, bf16[128,4096]{1,0:T(8,128)(2,1)S(1)} %copy-done.3, pred[128]{0:T(512)(128)(4,1)S(1)} %broadcast_compare_fusion), kind=kOutput, calls=%fused_computation.48 | convolution fusion | flops 807927808 | bytes 8798848 | tf_op jit(solution)/shard_map/dot_general | solution.py:34
  98.8 5.4 %fusion.43 = f32[128,768]{0,1:T(8,128)S(1)} fusion(bf16[4096,768]{1,0:T(8,128)(2,1)} %param.12, bf16[128,4096]{1,0:T(8,128)(2,1)S(1)} %copy-done.3, f32[4096]{0:T(1024)S(1)} %convert_element_type.83, f32[128]{0:T(128)S(1)} %get-tuple-element.45), kind=kOutput, calls=%fused_computation.49 | convolution fusion | flops 807403520 | bytes 7750144 | tf_op jit(solution)/shard_map/dot_general | solution.py:34
  105.5 49.8 %all-to-all-done = bf16[1,32,256,256]{3,2,0,1:T(8,128)(2,1)} async-done(((bf16[1,32,256,256]{3,2,0,1:T(8,128)(2,1)}), bf16[1,32,256,256]{3,2,0,1:T(8,128)(2,1)}, u32[]{:S(2)}, u32[]{:S(2)}) %all-to-all-start) | async-done | bytes 4194336 | tf_op jit(solution)/shard_map/all_to_all | solution.py:92
  155.3 6.9 %reshape.435 = bf16[8192,1,2,128]{3,2,0,1:T(2,128)(2,1)} reshape(bf16[1,32,256,256]{3,2,0,1:T(8,128)(2,1)} %all-to-all-done) | data formatting | bytes 8388608 | tf_op jit(solution)/shard_map/reshape | solution.py:94
  162.3 9.8 %fusion.95 = (bf16[8192,1,1,128]{3,2,0,1:T(2,128)(2,1)S(1)}, bf16[8192,1,1,128]{3,2,0,1:T(2,128)(2,1)}) fusion(bf16[8192,1,2,128]{3,2,0,1:T(2,128)(2,1)} %reshape.435), kind=kLoop, calls=%fused_computation.135 | loop fusion | bytes 8388608 | tf_op jit(solution)/shard_map/slice | solution.py:100
  172.1 8.3 %fusion.98 = (f32[4,128]{1,0:T(4,128)}, f32[1,4,128,8192]{3,2,1,0:T(8,128)}) fusion(bf16[8192,1,1,128]{3,2,0,1:T(2,128)(2,1)S(1)} %get-tuple-element.16, bf16[128,4,64]{2,0,1:T(8,128)(2,1)S(1)} %get-tuple-element.30, bf16[128,4,64]{2,0,1:T(8,128)(2,1)S(1)} %get-tuple-element.31, pred[8192]{0:T(1024)(128)(4,1)S(1)} %lt.48), kind=kOutput, calls=%fused_computation.138 | convolution fusion | flops 1086586368 | bytes 19015680 | tf_op jit(solution)/shard_map/bgqd,kgd->gqbk/dot_general | solution.py:49
  180.3 7.7 %fusion.100 = (f32[4,128]{1,0:T(4,128)S(1)}, f32[1,4,128,8192]{3,2,1,0:T(8,128)}) fusion(bf16[8192,1,1,128]{3,2,0,1:T(2,128)(2,1)S(1)} %get-tuple-element.16, bf16[128,4,64]{2,0,1:T(8,128)(2,1)S(1)} %get-tuple-element.19, bf16[128,4,64]{2,0,1:T(8,128)(2,1)S(1)} %get-tuple-element.18, pred[8192]{0:T(1024)(128)(4,1)S(1)} %lt.48), kind=kOutput, calls=%fused_computation.140 | convolution fusion | flops 1086586368 | bytes 19015680 | tf_op jit(solution)/shard_map/bgqd,kgd->gqbk/dot_general | solution.py:49
  188.0 8.3 %copy.114 = bf16[8192,1,1,128]{0,3,2,1:T(8,128)(2,1)S(1)} copy(bf16[8192,1,1,128]{3,2,0,1:T(2,128)(2,1)} %get-tuple-element.17) | data formatting | bytes 4194304
  196.4 8.9 %fusion.2 = f32[4,128]{1,0:T(4,128)S(1)} fusion(f32[1,4,128,8192]{3,2,1,0:T(8,128)} %get-tuple-element.37, f32[4,128]{1,0:T(4,128)S(1)} %max.18), kind=kLoop, calls=%fused_computation.9 | loop fusion | flops 8388096 | bytes 16781312 | tf_op jit(solution)/shard_map/reduce_sum | solution.py:60
  205.2 8.8 %fusion.26 = f32[128,4,128]{2,0,1:T(8,128)S(1)} fusion(bf16[8192,1,1,128]{0,3,2,1:T(8,128)(2,1)S(1)} %copy.114, f32[1,4,128,8192]{3,2,1,0:T(8,128)} %get-tuple-element.37, f32[4,128]{1,0:T(4,128)S(1)} %max.18), kind=kOutput, calls=%fused_computation.40 | convolution fusion | flops 1082130432 | bytes 19138560 | tf_op jit(solution)/shard_map/gqbk,kgd->bgqd/dot_general | solution.py:63
  214.0 8.4 %fusion.31 = f32[128,4,128]{2,0,1:T(8,128)S(1)} fusion(bf16[8192,1,1,128]{0,3,2,1:T(8,128)(2,1)} %copy-done.2, f32[1,4,128,8192]{3,2,1,0:T(8,128)} %get-tuple-element.41, f32[4,128]{1,0:T(4,128)S(1)} %max.19), kind=kOutput, calls=%fused_computation.41 | convolution fusion | flops 1082130432 | bytes 19138560 | tf_op jit(solution)/shard_map/gqbk,kgd->bgqd/dot_general | solution.py:63
  222.4 8.1 %fusion.4 = f32[4,128]{1,0:T(4,128)S(1)} fusion(f32[1,4,128,8192]{3,2,1,0:T(8,128)} %get-tuple-element.41, f32[4,128]{1,0:T(4,128)S(1)} %max.19), kind=kLoop, calls=%fused_computation.11 | loop fusion | flops 8388096 | bytes 16781312 | tf_op jit(solution)/shard_map/reduce_sum | solution.py:60
  230.6 0.9 fusion.38
  231.5 1.7 copy.99
  233.2 1.0 fusion.40
  (57 shorter events, 4.1 us)
Async XLA Ops:
  7.2 32.0 %copy-start = (bf16[2048,512]{1,0:T(8,128)(2,1)S(1)}, bf16[2048,512]{1,0:T(8,128)(2,1)}, u32[]{:S(2)}) copy-start(bf16[2048,512]{1,0:T(8,128)(2,1)} %param.13) | copy-start | bytes 6291460
  39.2 25.1 %copy-start.6 = (bf16[4096]{0:T(1024)(128)(2,1)S(1)}, bf16[4096]{0:T(1024)(128)(2,1)}, u32[]{:S(2)}) copy-start(bf16[4096]{0:T(1024)(128)(2,1)} %param.11) | copy-start | bytes 24580
  39.2 25.7 %copy-start.7 = (s32[1,32]{1,0:T(1,128)S(1)}, s32[1,32]{1,0:T(1,128)}, u32[]{:S(2)}) copy-start(s32[1,32]{1,0:T(1,128)} %param.15) | copy-start | bytes 388
  39.2 25.9 %copy-start.8 = (s32[128]{0:T(128)S(1)}, s32[128]{0:T(128)}, u32[]{:S(2)}) copy-start(s32[128]{0:T(128)} %param.19) | copy-start | bytes 1540
  39.2 51.6 %copy-start.3 = (bf16[128,4096]{1,0:T(8,128)(2,1)S(1)}, bf16[128,4096]{1,0:T(8,128)(2,1)}, u32[]{:S(2)}) copy-start(bf16[128,4096]{1,0:T(8,128)(2,1)} %param.10) | copy-start | bytes 3145732
  55.6 99.7 %all-to-all-start = ((bf16[1,32,256,256]{3,2,0,1:T(8,128)(2,1)}), bf16[1,32,256,256]{3,2,0,1:T(8,128)(2,1)}, u32[]{:S(2)}, u32[]{:S(2)}) async-start(bf16[1,32,256,256]{3,2,0,1:T(8,128)(2,1)} %bitcast.163), calls=%async_computation | async-start | bytes 8388608 | tf_op jit(solution)/shard_map/all_to_all | solution.py:92
  62.2 28.6 %all-gather.2.cloned.1.call-start = ((), (), s32[]{:S(2)}) async-start(), calls=%async_computation.3 | async-start | bytes 1179648 | tf_op jit(solution)/shard_map/all_gather | solution.py:118
  98.5 6.7 %copy-start.4 = (f32[128,768]{0,1:T(8,128)}, f32[128,768]{0,1:T(8,128)S(1)}, u32[]{:S(2)}) copy-start(f32[128,768]{0,1:T(8,128)S(1)} %fusion.41) | copy-start | bytes 1179652
  188.0 8.4 %copy-start.5 = (f32[4,128]{1,0:T(4,128)S(1)}, f32[4,128]{1,0:T(4,128)}, u32[]{:S(2)}) copy-start(f32[4,128]{1,0:T(4,128)} %get-tuple-element.36) | copy-start | bytes 6148
  196.4 8.9 %copy-start.2 = (bf16[8192,1,1,128]{0,3,2,1:T(8,128)(2,1)}, bf16[8192,1,1,128]{0,3,2,1:T(8,128)(2,1)S(1)}, u32[]{:S(2)}) copy-start(bf16[8192,1,1,128]{0,3,2,1:T(8,128)(2,1)S(1)} %copy.114) | copy-start | bytes 6291460
  214.0 21.0 %copy-start.1 = (bf16[2048,512]{1,0:T(8,128)(2,1)S(1)}, bf16[2048,512]{1,0:T(8,128)(2,1)}, u32[]{:S(2)}) copy-start(bf16[2048,512]{1,0:T(8,128)(2,1)} %param.13) | copy-start | bytes 6291460
Sparse Core Ops, SparseCore 0:
  65.5 25.3 all-gather.1
where the time goes:
time: 243 us; the launch traced here: 242 us
  waiting for transfers between devices  75.2 us (31%)
  matrix products  47.7 us (20%)
  local copies, waits for them, and re-layouts  42.5 us (17%)
  blocking collectives  34.2 us (14%)
  other arithmetic  20.6 us (8%)
  between operations  15 us (6%)
  starting transfers between devices  6.66 us (3%)
    all_to_all x1, waiting for transfers between devices, body(): lax.all_to_all(rotated_cache_pages, 'tok', split_axis=1, concat_axis=0, t...  49.8 us
    all_gather x1, waiting for transfers between devices, body(): full_rows = lax.all_gather(replacement, 'head', axis=1, tiled=True)  25.3 us
    all_to_all x1, blocking collectives, body(): lax.all_to_all(wanted, 'tok', split_axis=0, concat_axis=0, tiled=True)  19.1 us
    dot_general x2, matrix products, attend(): jnp.einsum('gqbk,kgd->bgqd', weights_cache, page_values, preferred_elemen...  17.1 us
    reduce_sum x4, other arithmetic, attend(): totals = jnp.sum(exp_cache, axis=-1) + jnp.sum(exp_block, axis=-1)  17.1 us
    dot_general x2, matrix products, attend(): jnp.einsum('bgqd,kgd->gqbk', query_vectors, page_keys, preferred_element_...  15.9 us
    all_to_all x1, blocking collectives, body(): lax.all_to_all(found_rows, 'tok', split_axis=0, concat_axis=0, tiled=True)  15.1 us
    unnamed x25, local copies, waits for them, and re-layouts  11.3 us
  transfers between devices with their start and end apart: 2, of which 2 were waited for; matrix products, arithmetic and copies ran while one was open for 7% of the time, Pallas kernels for 0%

commit v1 on v0

--- a/solution.py
+++ b/solution.py
@@ -115,7 +115,9 @@
     )
     returned = lax.all_to_all(found_rows, "tok", split_axis=0, concat_axis=0, tiled=True)
     replacement = returned[target_shard, slot_rank]
-    full_rows = lax.all_gather(replacement, "head", axis=1, tiled=True)
+    full_rows = jnp.concatenate(
+        lax.all_to_all(jnp.stack([replacement] * lax.axis_size("head")), "head", 0, 0), axis=1
+    )
     replaced = jnp.where(accept[:, None] == 1, full_rows, embeddings)
     queries_two, keys_two, values_two = project(
         replaced, norm_gain, query_key_value_weight, positions

time: 243 us -> 252 us (1.037); the launches traced: 242 us -> 247 us
  blocking collectives: 34.2 us -> 53.6 us
  between operations: 15 us -> 1.64 us
    all_to_all x1, waiting for transfers between devices: 49.8 us -> 76.4 us  [body(): lax.all_to_all(rotated_cache_pages, 'tok', split_axis=1, concat_axis=0, t...]
    all_gather x1 -> x0, waiting for transfers between devices: 25.3 us -> none  [body(): full_rows = lax.all_gather(replacement, 'head', axis=1, tiled=True)]
    all_to_all x0 -> x1, blocking collectives: none -> 19.4 us  [body(): lax.all_to_all(jnp.stack([replacement] * lax.axis_size('head')), 'head',...]
    unnamed x25 -> x24, local copies, waits for them, and re-layouts: 11.3 us -> 11.1 us
  transfers between devices with their start and end apart: 2 -> 1, of which waited for: 2 -> 1; matrix products, arithmetic and copies ran while one was open for 7% -> 6% of each run, Pallas kernels for 0% -> 0%
where the time goes in v1:
time: 252 us; the launch traced here: 247 us
  waiting for transfers between devices  76.4 us (30%)
  blocking collectives  53.6 us (21%)
  matrix products  46.7 us (19%)
  local copies, waits for them, and re-layouts  42.3 us (17%)
  other arithmetic  19.4 us (8%)
  starting transfers between devices  6.64 us (3%)
    all_to_all x1, waiting for transfers between devices, body(): lax.all_to_all(rotated_cache_pages, 'tok', split_axis=1, concat_axis=0, t...  76.4 us
    all_to_all x1, blocking collectives, body(): lax.all_to_all(jnp.stack([replacement] * lax.axis_size('head')), 'head',...  19.4 us
    all_to_all x1, blocking collectives, body(): lax.all_to_all(wanted, 'tok', split_axis=0, concat_axis=0, tiled=True)  19.1 us
    reduce_sum x4, other arithmetic, attend(): totals = jnp.sum(exp_cache, axis=-1) + jnp.sum(exp_block, axis=-1)  17.1 us
    dot_general x2, matrix products, attend(): jnp.einsum('gqbk,kgd->bgqd', weights_cache, page_values, preferred_elemen...  16.9 us
    dot_general x2, matrix products, attend(): jnp.einsum('bgqd,kgd->gqbk', query_vectors, page_keys, preferred_element_...  15.4 us
    all_to_all x1, blocking collectives, body(): lax.all_to_all(found_rows, 'tok', split_axis=0, concat_axis=0, tiled=True)  15.1 us
    dot_general x2, matrix products, project(): jnp.dot(normed, query_key_value_weight, preferred_element_type=jnp.float32)  11.6 us
  transfers between devices with their start and end apart: 1, of which 1 were waited for; matrix products, arithmetic and copies ran while one was open for 6% of the time, Pallas kernels for 0%

profile of v1, /device:TPU:12, one launch (start us, length us, event | category | flops | bytes accessed | tf_op | source)
XLA Modules:
  0.0 246.7 jit_solution(9440197627094265780)
XLA Ops:
  0.6 1.0 fusion.36
  1.6 0.7 fusion.89
  2.3 10.9 %scatter_fusion = s32[32,8]{0,1:T(8,128)S(1)} fusion(s32[32,8]{0,1:T(8,128)S(1)} %broadcast_in_dim.55, s32[128]{0:T(128)S(1)} %get-tuple-element.16, s32[128]{0:T(128)} %param.18), kind=kCustom, calls=%fused_computation.2 | custom fusion | bytes 2560 | tf_op jit(solution)/shard_map/scatter | solution.py:112
  13.3 19.1 %all_to_all.34 = s32[32,1,8]{2,1,0:T(1,128)S(1)} all-to-all(s32[32,1,8]{2,1,0:T(1,128)S(1)} %copy.118), channel_id=1, replica_groups=mesh['tok'=32,'head'=8] {'tok'}, dimensions={0} | all-to-all | bytes 2048 | tf_op jit(solution)/shard_map/all_to_all | solution.py:114
  32.7 1.2 gather_fusion
  33.9 15.1 %all_to_all.35 = bf16[32,8,512]{2,1,0:T(8,128)(2,1)S(1)} all-to-all(bf16[32,8,512]{2,1,0:T(8,128)(2,1)S(1)} %bitcast_select_fusion.3), channel_id=1, replica_groups=mesh['tok'=32,'head'=8] {'tok'}, dimensions={0} | all-to-all | bytes 524288 | tf_op jit(solution)/shard_map/all_to_all | solution.py:116
  49.0 1.3 gather_fusion.1
  50.5 19.4 %all_to_all.36 = bf16[8,128,512]{2,1,0:T(8,128)(2,1)S(1)} all-to-all(bf16[8,128,512]{2,1,0:T(8,128)(2,1)S(1)} %stack.2), channel_id=1, replica_groups=mesh['tok'=32,'head'=8] {'head'}, dimensions={0} | all-to-all | bytes 2097152 | tf_op jit(solution)/shard_map/all_to_all | solution.py:119
  69.9 6.6 %all-to-all-start = ((bf16[1,32,256,256]{3,2,0,1:T(8,128)(2,1)}), bf16[1,32,256,256]{3,2,0,1:T(8,128)(2,1)}, u32[]{:S(2)}, u32[]{:S(2)}) async-start(bf16[1,32,256,256]{3,2,0,1:T(8,128)(2,1)} %bitcast.168), calls=%async_computation | async-start | bytes 8388608 | tf_op jit(solution)/shard_map/all_to_all | solution.py:92
  79.8 5.8 %fusion.41 = f32[128,768]{0,1:T(8,128)S(1)} fusion(bf16[4096,768]{1,0:T(8,128)(2,1)} %param.12, bf16[128,4096]{0,1:T(8,128)(2,1)S(1)} %get-tuple-element.15, f32[128]{0:T(128)S(1)} %get-tuple-element.47, f32[4096]{0:T(1024)S(1)} %convert_element_type.83), kind=kOutput, calls=%fused_computation.48 | convolution fusion | flops 807403520 | bytes 7750144 | tf_op jit(solution)/shard_map/dot_general | solution.py:34
  85.9 5.8 %fusion.43 = f32[128,768]{0,1:T(8,128)S(1)} fusion(bf16[4096,768]{1,0:T(8,128)(2,1)} %param.12, bf16[128,4096]{0,1:T(8,128)(2,1)S(1)} %copy.109, f32[4096]{0:T(1024)S(1)} %convert_element_type.83, f32[128]{0:T(128)S(1)} %get-tuple-element.48), kind=kOutput, calls=%fused_computation.49 | convolution fusion | flops 807403520 | bytes 7750144 | tf_op jit(solution)/shard_map/dot_general | solution.py:34
  93.0 76.4 %all-to-all-done = bf16[1,32,256,256]{3,2,0,1:T(8,128)(2,1)} async-done(((bf16[1,32,256,256]{3,2,0,1:T(8,128)(2,1)}), bf16[1,32,256,256]{3,2,0,1:T(8,128)(2,1)}, u32[]{:S(2)}, u32[]{:S(2)}) %all-to-all-start) | async-done | bytes 4194336 | tf_op jit(solution)/shard_map/all_to_all | solution.py:92
  169.4 6.9 %reshape.445 = bf16[8192,1,2,128]{3,2,0,1:T(2,128)(2,1)} reshape(bf16[1,32,256,256]{3,2,0,1:T(8,128)(2,1)} %all-to-all-done) | data formatting | bytes 8388608 | tf_op jit(solution)/shard_map/reshape | solution.py:94
  176.3 9.8 %fusion.95 = (bf16[8192,1,1,128]{3,2,0,1:T(2,128)(2,1)S(1)}, bf16[8192,1,1,128]{3,2,0,1:T(2,128)(2,1)}) fusion(bf16[8192,1,2,128]{3,2,0,1:T(2,128)(2,1)} %reshape.445), kind=kLoop, calls=%fused_computation.135 | loop fusion | bytes 8388608 | tf_op jit(solution)/shard_map/slice | solution.py:100
  186.1 7.7 %fusion.98 = (f32[4,128]{1,0:T(4,128)S(1)}, f32[1,4,128,8192]{3,2,1,0:T(8,128)}) fusion(bf16[8192,1,1,128]{3,2,0,1:T(2,128)(2,1)S(1)} %get-tuple-element.18, bf16[128,4,64]{2,0,1:T(8,128)(2,1)S(1)} %get-tuple-element.33, bf16[128,4,64]{2,0,1:T(8,128)(2,1)S(1)} %get-tuple-element.34, pred[8192]{0:T(1024)(128)(4,1)S(1)} %lt.48), kind=kOutput, calls=%fused_computation.138 | convolution fusion | flops 1086586368 | bytes 19015680 | tf_op jit(solution)/shard_map/bgqd,kgd->gqbk/dot_general | solution.py:49
  193.8 7.7 %fusion.100 = (f32[4,128]{1,0:T(4,128)S(1)}, f32[1,4,128,8192]{3,2,1,0:T(8,128)}) fusion(bf16[8192,1,1,128]{3,2,0,1:T(2,128)(2,1)S(1)} %get-tuple-element.18, bf16[128,4,64]{2,0,1:T(8,128)(2,1)S(1)} %get-tuple-element.22, bf16[128,4,64]{2,0,1:T(8,128)(2,1)S(1)} %get-tuple-element.21, pred[8192]{0:T(1024)(128)(4,1)S(1)} %lt.48), kind=kOutput, calls=%fused_computation.140 | convolution fusion | flops 1086586368 | bytes 19015680 | tf_op jit(solution)/shard_map/bgqd,kgd->gqbk/dot_general | solution.py:49
  201.5 8.3 %copy.143 = bf16[8192,1,1,128]{0,3,2,1:T(8,128)(2,1)S(1)} copy(bf16[8192,1,1,128]{3,2,0,1:T(2,128)(2,1)} %get-tuple-element.19) | data formatting | bytes 4194304
  209.8 8.9 %fusion.2 = f32[4,128]{1,0:T(4,128)S(1)} fusion(f32[1,4,128,8192]{3,2,1,0:T(8,128)} %get-tuple-element.40, f32[4,128]{1,0:T(4,128)S(1)} %max.18), kind=kLoop, calls=%fused_computation.9 | loop fusion | flops 8388096 | bytes 16781312 | tf_op jit(solution)/shard_map/reduce_sum | solution.py:60
  218.7 8.8 %fusion.26 = f32[128,4,128]{2,0,1:T(8,128)S(1)} fusion(bf16[8192,1,1,128]{0,3,2,1:T(8,128)(2,1)S(1)} %copy.143, f32[1,4,128,8192]{3,2,1,0:T(8,128)} %get-tuple-element.40, f32[4,128]{1,0:T(4,128)S(1)} %max.18), kind=kOutput, calls=%fused_computation.40 | convolution fusion | flops 1082130432 | bytes 19138560 | tf_op jit(solution)/shard_map/gqbk,kgd->bgqd/dot_general | solution.py:63
  227.5 8.2 %fusion.31 = f32[128,4,128]{2,0,1:T(8,128)S(1)} fusion(bf16[8192,1,1,128]{0,3,2,1:T(8,128)(2,1)} %copy-done.2, f32[1,4,128,8192]{3,2,1,0:T(8,128)} %get-tuple-element.44, f32[4,128]{1,0:T(4,128)S(1)} %max.19), kind=kOutput, calls=%fused_computation.41 | convolution fusion | flops 1082130432 | bytes 19138560 | tf_op jit(solution)/shard_map/gqbk,kgd->bgqd/dot_general | solution.py:63
  235.7 8.1 %fusion.4 = f32[4,128]{1,0:T(4,128)S(1)} fusion(f32[1,4,128,8192]{3,2,1,0:T(8,128)} %get-tuple-element.44, f32[4,128]{1,0:T(4,128)S(1)} %max.19), kind=kLoop, calls=%fused_computation.11 | loop fusion | flops 8388096 | bytes 16781312 | tf_op jit(solution)/shard_map/reduce_sum | solution.py:60
  243.9 1.0 fusion.38
  244.9 0.8 copy.128
  246.0 0.8 copy.129
  (56 shorter events, 4.9 us)
Async XLA Ops:
  0.6 32.0 %copy-start = (bf16[2048,512]{1,0:T(8,128)(2,1)S(1)}, bf16[2048,512]{1,0:T(8,128)(2,1)}, u32[]{:S(2)}) copy-start(bf16[2048,512]{1,0:T(8,128)(2,1)} %param.13) | copy-start | bytes 6291460
  49.0 27.5 %copy-start.3 = (bf16[128,4096]{1,0:T(8,128)(2,1)S(1)}, bf16[128,4096]{1,0:T(8,128)(2,1)}, u32[]{:S(2)}) copy-start(bf16[128,4096]{1,0:T(8,128)(2,1)} %param.10) | copy-start | bytes 3145732
  50.4 26.8 %copy-start.5 = (bf16[4096]{0:T(1024)(128)(2,1)S(1)}, bf16[4096]{0:T(1024)(128)(2,1)}, u32[]{:S(2)}) copy-start(bf16[4096]{0:T(1024)(128)(2,1)} %param.11) | copy-start | bytes 24580
  50.4 27.5 %copy-start.6 = (s32[1,32]{1,0:T(1,128)S(1)}, s32[1,32]{1,0:T(1,128)}, u32[]{:S(2)}) copy-start(s32[1,32]{1,0:T(1,128)} %param.15) | copy-start | bytes 388
  50.4 27.7 %copy-start.7 = (s32[128]{0:T(128)S(1)}, s32[128]{0:T(128)}, u32[]{:S(2)}) copy-start(s32[128]{0:T(128)} %param.19) | copy-start | bytes 1540
  69.9 99.5 %all-to-all-start = ((bf16[1,32,256,256]{3,2,0,1:T(8,128)(2,1)}), bf16[1,32,256,256]{3,2,0,1:T(8,128)(2,1)}, u32[]{:S(2)}, u32[]{:S(2)}) async-start(bf16[1,32,256,256]{3,2,0,1:T(8,128)(2,1)} %bitcast.168), calls=%async_computation | async-start | bytes 8388608 | tf_op jit(solution)/shard_map/all_to_all | solution.py:92
  91.7 84.6 %copy-start.4 = (f32[128,768]{0,1:T(8,128)}, f32[128,768]{0,1:T(8,128)S(1)}, u32[]{:S(2)}) copy-start(f32[128,768]{0,1:T(8,128)S(1)} %fusion.43) | copy-start | bytes 1179652
  209.8 8.9 %copy-start.2 = (bf16[8192,1,1,128]{0,3,2,1:T(8,128)(2,1)}, bf16[8192,1,1,128]{0,3,2,1:T(8,128)(2,1)S(1)}, u32[]{:S(2)}) copy-start(bf16[8192,1,1,128]{0,3,2,1:T(8,128)(2,1)S(1)} %copy.143) | copy-start | bytes 6291460
  227.5 19.2 %copy-start.1 = (bf16[2048,512]{1,0:T(8,128)(2,1)S(1)}, bf16[2048,512]{1,0:T(8,128)(2,1)}, u32[]{:S(2)}) copy-start(bf16[2048,512]{1,0:T(8,128)(2,1)} %param.13) | copy-start | bytes 6291460
